TPU v7x, 32 devices: a whole 2x2x4 slice. The times are simulated.
32 devices in a mesh: lon: 4 (over x, core), lat: 8 (over z, y).
Axes of the slice: x: 2, y: 2, z: 4, core: 2. Of those that a mesh axis runs over, the one named last changes fastest.
Arguments:
- prognostic: float32 [4, 16, 192, 1536], P(None, None, 'lat', 'lon'), may hold values from -6 to 6
- tracers: float32 [4, 16, 192, 1536], P(None, None, 'lat', 'lon'), may hold values from -6 to 6
- zonal_courant: float32 [16, 192, 1536], P(None, 'lat', 'lon'), may hold values from -0.45 to 0.45
- meridional_courant: float32 [16, 192, 1536], P(None, 'lat', 'lon'), may hold values from -0.45 to 0.45
- filter_band: int32 [192], P('lat'), may hold values from 96 to 768, as said below
- dep_owner: int32 [192, 2], P('lat'), may hold values from 0 to 7, as said below
- dep_row: int32 [192, 2], P('lat'), may hold values from 0 to 23
- dep_weight: float32 [192, 2], P('lat'), may hold values from 0 to 1, as said below
Outputs:
- new_prognostic: float32 [4, 16, 192, 1536], P(None, None, 'lat', 'lon')
- new_tracers: float32 [4, 16, 192, 1536], P(None, None, 'lat', 'lon')
Inputs may be any that keep to these rules, and one draw needn't show every extreme that they name: `filter_band`: rows within 24 of either pole hold values below 768; all other rows hold 768. `dep_owner`: among the 48 entries of one band, at most 12 name the same owner band, and some owner is named exactly 12 times; the owners a band names are the bands nearest to it, distance counted across either pole. `dep_weight`: Positive; the 2 weights of a row sum to 1.
All inputs are finite; a program needn't handle non-finite values.
Results may differ from a plain program's by a relative error of at most 0.00007.
Values sent between devices are 32-bit elements; how exact they have to be, the bound alone decides.
No kernel may reach another device: no remote copies, remote signals or barrier semaphores. Data moves between devices by JAX's collectives and lax.ppermute only.
A program may use at most 128 MiB of HBM per device.

v0:
```python
import math
import jax
import jax.numpy as jnp
from jax import lax
from jax.sharding import PartitionSpec as P

PRECISE = lax.Precision.HIGHEST


def padded(value, sides, width, wrap):
    for axis, dim in sides:
        size, length = (lax.axis_size(axis), value.shape[dim])
        up = [(i, (i + 1) % size) for i in range(size if wrap else size - 1)]
        down = [(j, i) for i, j in up]
        last = lax.slice_in_dim(value, length - width, length, axis=dim)
        first = lax.slice_in_dim(value, 0, width, axis=dim)
        before = lax.ppermute(last, axis, up)
        after = lax.ppermute(first, axis, down)
        value = jnp.concatenate([before, value, after], axis=dim)
    return value


def face_flux(values, speeds, axis):
    count = values.shape[axis] - 2
    left_cells = lax.slice_in_dim(values, 0, count + 1, axis=axis)
    right_cells = lax.slice_in_dim(values, 1, count + 2, axis=axis)
    courant = lax.slice_in_dim(speeds, 0, count + 1, axis=axis)
    return 0.5 * courant * (left_cells + right_cells) - 0.5 * courant * courant * (
        right_cells - left_cells
    )


def real_basis(first_cell, count, length):
    cells = first_cell + jnp.arange(count, dtype=jnp.int32)
    column = jnp.arange(length, dtype=jnp.int32)
    half_length = length // 2
    frequency = jnp.where(column <= half_length, column, column - half_length)
    phase_index = cells[:, None] * frequency[None, :] % length
    angles = 2.0 * math.pi / length * phase_index.astype(jnp.float32)
    return jnp.where((column <= half_length)[None, :], jnp.cos(angles), jnp.sin(angles))


def column_factors(band_rows, length):
    column = jnp.arange(length, dtype=jnp.int32)
    half_length = length // 2
    frequency = jnp.where(column <= half_length, column, column - half_length)
    single = (column == 0) | (column == half_length)
    weights = jnp.where(single, 1.0 / length, 2.0 / length).astype(jnp.float32)
    ratios = (
        band_rows.astype(jnp.float32)[:, None]
        / jnp.maximum(frequency, 1).astype(jnp.float32)[None, :]
    )
    damping = jnp.minimum(1.0, ratios * ratios)
    return (damping - 1.0) * weights[None, :]


def polar_filter(values, band_rows):
    block_cells = values.shape[3]
    length = block_cells * lax.axis_size("lon")
    basis_table = real_basis(lax.axis_index("lon") * block_cells, block_cells, length)
    needed = jnp.any(band_rows < length // 2)

    def forward(grid):
        return jnp.einsum("flrn,nk->flrk", grid, basis_table, precision=PRECISE)

    def nothing(grid):
        return jnp.zeros(grid.shape[:3] + (length,), jnp.float32)

    partial_spec = lax.cond(needed, forward, nothing, values)
    spectrum = lax.psum(partial_spec, "lon")
    factors = column_factors(band_rows, length)

    def inverse(coeffs):
        return jnp.einsum(
            "flrk,nk->flrn", coeffs * factors[None, None], basis_table, precision=PRECISE
        )

    def no_change(coeffs):
        return jnp.zeros(coeffs.shape[:3] + (block_cells,), jnp.float32)

    return values + lax.cond(needed, inverse, no_change, spectrum)


def departure_terms(tracers, dep_owner, dep_row, dep_weight):
    band_count = lax.axis_size("lat")
    row_count, link_count = dep_owner.shape
    entries = row_count * link_count
    capacity = max(2, -(-2 * entries // band_count))
    owner_ids = dep_owner.reshape(entries)
    source = dep_row.reshape(entries)
    positions = jnp.arange(entries)
    earlier = (owner_ids[:, None] == owner_ids[None, :]) & (positions[None, :] < positions[:, None])
    slot_ids = jnp.sum(earlier.astype(jnp.int32), axis=1)
    band_ids = jnp.arange(band_count, dtype=jnp.int32)
    slot_range = jnp.arange(capacity, dtype=jnp.int32)
    matches = (owner_ids[:, None, None] == band_ids[None, :, None]) & (
        slot_ids[:, None, None] == slot_range[None, None, :]
    )
    request = jnp.sum(jnp.where(matches, source[:, None, None], 0), axis=0)
    wanted = lax.all_to_all(request, "lat", split_axis=0, concat_axis=0, tiled=True)
    by_row = jnp.transpose(tracers, (2, 0, 1, 3))
    outgoing = by_row[wanted]
    incoming = lax.all_to_all(outgoing, "lat", split_axis=0, concat_axis=0, tiled=True)
    stacked_rows = incoming.reshape((band_count * capacity,) + incoming.shape[2:])
    picked = stacked_rows[owner_ids * capacity + slot_ids].reshape(
        (row_count, link_count) + stacked_rows.shape[1:]
    )
    summed = dep_weight[:, 0][:, None, None, None] * picked[:, 0]
    summed = summed + dep_weight[:, 1][:, None, None, None] * picked[:, 1]
    return jnp.transpose(summed, (1, 2, 0, 3))


def body(
    prognostic,
    tracers,
    zonal_courant,
    meridional_courant,
    filter_band,
    dep_owner,
    dep_row,
    dep_weight,
):
    row_count = prognostic.shape[2]
    departed = departure_terms(tracers, dep_owner, dep_row, dep_weight)
    lon_padded = padded(
        jnp.concatenate([prognostic, zonal_courant[None]], axis=0), (("lon", 3),), 1, True
    )
    zonal_flux = face_flux(lon_padded[:-1], lon_padded[-1:], 3)
    lat_padded = padded(
        jnp.concatenate([prognostic, meridional_courant[None]], axis=0), (("lat", 2),), 1, False
    )
    merid_flux = face_flux(lat_padded[:-1], lat_padded[-1:], 2)
    total_rows = row_count * lax.axis_size("lat")
    face_rows = lax.axis_index("lat") * row_count + jnp.arange(row_count + 1) - 1
    merid_flux = jnp.where(
        (face_rows == total_rows - 1)[None, None, :, None], jnp.float32(0.0), merid_flux
    )
    advected = (
        prognostic
        - (zonal_flux[..., 1:] - zonal_flux[..., :-1])
        - (merid_flux[:, :, 1:] - merid_flux[:, :, :-1])
    )
    new_prognostic = polar_filter(advected, filter_band)
    return (new_prognostic, departed)


def solution(mesh):
    return jax.shard_map(
        body,
        mesh=mesh,
        in_specs=(
            P(None, None, "lat", "lon"),
            P(None, None, "lat", "lon"),
            P(None, "lat", "lon"),
            P(None, "lat", "lon"),
            P("lat"),
            P("lat", None),
            P("lat", None),
            P("lat", None),
        ),
        out_specs=(P(None, None, "lat", "lon"), P(None, None, "lat", "lon")),
        check_vma=False,
    )
```

profile of v0, /device:TPU:0, one launch (start us, length us, event | category | flops | bytes accessed | tf_op | source)
XLA Modules:
  0.0 461.9 jit_solution(5204649697896423825)
XLA Ops:
  7.2 0.8 copy.66
  7.9 0.1 eq.76
  8.0 0.2 convert_reduce_fusion
  8.2 0.8 copy.67
  9.0 0.1 broadcast_in_dim.68
  9.1 0.3 select_reduce_fusion
  9.4 0.7 copy.69
  10.1 7.3 %all-to-all-start = ((s32[8,1,12]{2,1,0:T(1,128)}), s32[8,1,12]{2,1,0:T(1,128)S(1)}, u32[]{:S(2)}, u32[]{:S(2)}) async-start(s32[8,1,12]{2,1,0:T(1,128)} %copy.69), calls=%async_computation | async-start | bytes 8192 | tf_op jit(solution)/shard_map/all_to_all | solution.py:100
  17.3 2.1 copy.83
  19.5 4.3 all-to-all-done
  23.7 0.1 reshape.169
  23.8 4.8 %gather_fusion = f32[96,4,16,384]{3,2,1,0:T(8,128)} fusion(f32[24,4,16,384]{3,2,1,0:T(8,128)S(1)} %bitcast.59, s32[1024]{0:T(1024)S(1)} %pad_clamp_fusion.1), kind=kCustom, calls=%fused_computation | custom fusion | bytes 18874752 | tf_op jit(solution)/shard_map/gather | solution.py:102
  28.6 5.3 %all-to-all-start.1 = ((f32[8,12,4,16,384]{4,3,2,1,0:T(8,128)}), f32[8,12,4,16,384]{4,3,2,1,0:T(8,128)}, u32[]{:S(2)}, u32[]{:S(2)}) async-start(f32[8,12,4,16,384]{4,3,2,1,0:T(8,128)} %bitcast.60), calls=%async_computation.1 | async-start | bytes 18874368 | tf_op jit(solution)/shard_map/all_to_all | solution.py:103
  34.0 0.2 pad_maximum_fusion.11
  34.2 4.4 collective-permute-start.2
  38.6 0.7 copy.80
  39.3 1.3 collective-permute-start.3
  40.6 1.6 pad_maximum_fusion.8
  42.1 1.7 copy.77
  43.9 1.7 copy.78
  45.6 1.8 collective-permute-start.1
  47.4 0.6 compare_reduce_fusion
  48.1 10.9 %sine_select_fusion = f32[384,1536]{1,0:T(8,128)} fusion(s32[1536]{0:T(1024)S(1)} %add_select_fusion.1, s32[384]{0:T(512)S(1)} %iota_add_fusion, pred[1536]{0:T(1024)(128)(4,1)S(1)} %iota_compare_fusion.2), kind=kLoop, calls=%fused_computation.42 | loop fusion | flops 5898240 | bytes 2368512 | tf_op jit(solution)/shard_map/jit(_where)/select_n | solution.py:40
  59.6 0.5 copy.58
  60.1 2.3 copy.60
  62.4 1.5 multiply_bitcast_fusion.1
  63.8 0.1 fusion.22
  64.0 1.5 multiply_subtract_fusion
  65.4 49.1 %collective-permute-done.2 = f32[5,16,1,384]{3,1,2,0:T(8,128)} collective-permute-done((f32[5,16,1,384]{3,1,2,0:T(8,128)S(1)}, f32[5,16,1,384]{3,1,2,0:T(8,128)}, u32[]{:S(2)}, u32[]{:S(2)}) %collective-permute-start.2) | collective-permute-done | bytes 122912 | tf_op jit(solution)/shard_map/ppermute | solution.py:17
  114.5 1.0 copy.62
  115.6 1.0 copy.64
  116.6 0.2 multiply_bitcast_fusion
  116.8 0.1 fusion.23
  116.9 1.2 subtract_select_fusion
  118.0 2.3 fusion.16
  120.3 20.0 %conditional.2 = (f32[4,16,24,1536]{3,2,1,0:T(8,128)}) conditional(s32[]{:T(128)} %convert_element_type.23, () %tuple.57, (f32[4,16,24,384]{3,2,1,0:T(8,128)}, f32[384,1536]{1,0:T(8,128)}) %tuple.58), branch_computations={%region_1.2_spmd, %region_2.3_spmd} | conditional | flops 10871635968 | bytes 14155784 | solution.py:69
  120.3 20.0 %fusion = f32[4,16,24,1536]{3,2,1,0:T(8,128)} fusion(f32[4,16,24,384]{3,2,1,0:T(8,128)} %get-tuple-element.63, f32[384,1536]{1,0:T(8,128)} %get-tuple-element.64), kind=kOutput, calls=%fused_computation.2 | convolution fusion | flops 10871635968 | bytes 14155776 | tf_op jit(solution)/shard_map/cond/branch_1_fun/flrn,nk->flrk/dot_general | solution.py:64
  140.3 0.6 copy-done.10
  141.0 0.1 copy.70
  141.1 0.1 mul.173
  141.2 278.5 %all-reduce.2.cloned.1.call-done = f32[4,16,24,1536]{3,2,1,0:T(8,128)} async-done(((f32[4,16,24,1536]{3,2,1,0:T(8,128)}), f32[4,16,24,1536]{3,2,1,0:T(8,128)}) %all-reduce.2.cloned.1.call-update) | async-done | bytes 9437200 | tf_op jit(solution)/shard_map/psum | solution.py:70
  419.8 19.6 %conditional.3 = (f32[4,16,24,384]{3,2,1,0:T(8,128)}) conditional(s32[]{:T(128)} %convert_element_type.23, () %tuple.56, (f32[24]{0:T(128)S(1)}, f32[1,1536]{1,0:T(1,128)S(1)}, s32[1,1536]{1,0:T(1,128)S(1)}, s32[1,1536]{1,0:T(1,128)S(1)}, f32[4,16,24,1536]{3,2,1,0:T(8,128)}, /*index=5*/f32[384,1536]{1,0:T(8,128)}) %tuple.59), branch_computations={%region_4.5_spmd, %region_5.6_spmd} | conditional | flops 10874185728 | bytes 14493804 | solution.py:81
  420.1 0.1 fusion.8
  420.2 19.2 %fusion.2 = f32[4,16,24,384]{3,2,1,0:T(8,128)} fusion(f32[4,16,24,1536]{3,2,1,0:T(8,128)} %get-tuple-element.65, f32[24,1536]{1,0:T(8,128)S(1)} %fusion.8, f32[384,1536]{1,0:T(8,128)} %get-tuple-element.70), kind=kOutput, calls=%fused_computation.4 | convolution fusion | flops 10873995264 | bytes 14303232 | tf_op jit(solution)/shard_map/cond/branch_1_fun/flrk,nk->flrn/dot_general | solution.py:74
  439.3 3.3 add.102
  442.6 6.8 %gather_fusion.1 = f32[48,4,16,384]{3,2,1,0:T(8,128)} fusion(f32[96,4,16,384]{3,2,1,0:T(8,128)} %bitcast.15, s32[1024]{0:T(1024)S(1)} %pad_clamp_fusion), kind=kCustom, calls=%fused_computation.1 | custom fusion | bytes 9437376 | tf_op jit(solution)/shard_map/gather | solution.py:105
  449.4 2.9 fusion.14
  452.3 2.8 copy.72
  (47 shorter events, 0.3 us)
Async XLA Ops:
  10.1 13.7 %all-to-all-start = ((s32[8,1,12]{2,1,0:T(1,128)}), s32[8,1,12]{2,1,0:T(1,128)S(1)}, u32[]{:S(2)}, u32[]{:S(2)}) async-start(s32[8,1,12]{2,1,0:T(1,128)} %copy.69), calls=%async_computation | async-start | bytes 8192 | tf_op jit(solution)/shard_map/all_to_all | solution.py:100
  28.6 5.4 %copy-start = (f32[4,16,24,384]{3,2,1,0:T(8,128)S(1)}, f32[4,16,24,384]{3,2,1,0:T(8,128)}, u32[]{:S(2)}) copy-start(f32[4,16,24,384]{3,2,1,0:T(8,128)} %param.12) | copy-start | bytes 7077892
  28.6 5.4 %copy-start.4 = (f32[16,24,384]{2,1,0:T(8,128)S(1)}, f32[16,24,384]{2,1,0:T(8,128)}, u32[]{:S(2)}) copy-start(f32[16,24,384]{2,1,0:T(8,128)} %param.15) | copy-start | bytes 1769476
  28.6 414.0 %all-to-all-start.1 = ((f32[8,12,4,16,384]{4,3,2,1,0:T(8,128)}), f32[8,12,4,16,384]{4,3,2,1,0:T(8,128)}, u32[]{:S(2)}, u32[]{:S(2)}) async-start(f32[8,12,4,16,384]{4,3,2,1,0:T(8,128)} %bitcast.60), calls=%async_computation.1 | async-start | bytes 18874368 | tf_op jit(solution)/shard_map/all_to_all | solution.py:103
  33.9 6.6 %copy-start.2 = (f32[16,24,384]{2,1,0:T(8,128)S(1)}, f32[16,24,384]{2,1,0:T(8,128)}, u32[]{:S(2)}) copy-start(f32[16,24,384]{2,1,0:T(8,128)} %param.14) | copy-start | bytes 1769476
  34.0 385.8 %all-reduce.2.cloned.1.call-start = ((), (), s32[]{:S(2)}) async-start(), calls=%async_computation.2 | async-start | bytes 18874368 | tf_op jit(solution)/shard_map/psum | solution.py:70
  34.2 80.3 %collective-permute-start.2 = (f32[5,16,1,384]{3,1,2,0:T(8,128)S(1)}, f32[5,16,1,384]{3,1,2,0:T(8,128)}, u32[]{:S(2)}, u32[]{:S(2)}) collective-permute-start(f32[5,16,1,384]{3,1,2,0:T(8,128)S(1)} %copy.79), channel_id=1, source_target_pairs={{0,1},{1,2},{2,3},{3,4},{4,5},{5,6},{6,7},{8,9},{9,10},{10,11},{11... | collective-permute-start | bytes 368648 | tf_op jit(solution)/shard_map/ppermute | solution.py:17
  39.3 76.3 %collective-permute-start.3 = (f32[5,16,1,384]{3,1,2,0:T(8,128)}, f32[5,16,1,384]{3,1,2,0:T(8,128)}, u32[]{:S(2)}, u32[]{:S(2)}) collective-permute-start(f32[5,16,1,384]{3,1,2,0:T(8,128)} %copy.80), channel_id=1, source_target_pairs={{1,0},{2,1},{3,2},{4,3},{5,4},{6,5},{7,6},{9,8},{10,9},{11,10},{12... | collective-permute-start | bytes 368648 | tf_op jit(solution)/shard_map/ppermute | solution.py:18
  40.6 6.9 %copy-start.9 = (s32[24]{0:T(128)S(1)}, s32[24]{0:T(128)}, u32[]{:S(2)}) copy-start(s32[24]{0:T(128)} %param.16) | copy-start | bytes 292
  43.9 15.7 %collective-permute-start = (f32[5,16,24,1]{2,1,3,0:T(8,128)S(1)}, f32[5,16,24,1]{2,1,3,0:T(8,128)S(1)}, u32[]{:S(2)}, u32[]{:S(2)}) collective-permute-start(f32[5,16,24,1]{2,1,3,0:T(8,128)S(1)} %copy.77), channel_id=1, source_target_pairs={{0,8},{8,16},{16,24},{24,0},{1,9},{9,17},{17,25},{25,1},{2,10},{10... | collective-permute-start | bytes 23048 | tf_op jit(solution)/shard_map/ppermute | solution.py:17
  45.6 14.5 %collective-permute-start.1 = (f32[5,16,24,1]{2,1,3,0:T(8,128)S(1)}, f32[5,16,24,1]{2,1,3,0:T(8,128)}, u32[]{:S(2)}, u32[]{:S(2)}) collective-permute-start(f32[5,16,24,1]{2,1,3,0:T(8,128)S(1)} %copy.78), channel_id=1, source_target_pairs={{8,0},{16,8},{24,16},{0,24},{9,1},{17,9},{25,17},{1,25},{10,2},{18... | collective-permute-start | bytes 23048 | tf_op jit(solution)/shard_map/ppermute | solution.py:18
  62.4 1.6 copy-start.3
  62.4 1.6 copy-start.6
  64.0 52.6 %copy-start.5 = (f32[16,24,384]{2,1,0:T(8,128)S(1)}, f32[16,24,384]{2,1,0:T(8,128)}, u32[]{:S(2)}) copy-start(f32[16,24,384]{2,1,0:T(8,128)} %param.15) | copy-start | bytes 1769476
  140.3 0.7 copy-start.10
  140.3 0.7 copy-start.7
  140.3 0.9 copy-start.8
  419.8 19.6 %copy-start.1 = (f32[4,16,24,384]{3,2,1,0:T(8,128)S(1)}, f32[4,16,24,384]{3,2,1,0:T(8,128)}, u32[]{:S(2)}) copy-start(f32[4,16,24,384]{3,2,1,0:T(8,128)} %fusion.16) | copy-start | bytes 7077892
Sparse Core Ops, SparseCore 0:
  140.4 279.2 all-reduce.1
where the time goes:
time: 463 us; the launch traced here: 462 us
  waiting for transfers between devices  332 us (72%)
  matrix products  39.1 us (8%)
  local copies, waits for them, and re-layouts  28.8 us (6%)
  other arithmetic  26.8 us (6%)
  starting transfers between devices  20.1 us (4%)
  between operations  15 us (3%)
    psum x1, waiting for transfers between devices, polar_filter(): spectrum = lax.psum(partial_spec, 'lon')  279 us
    ppermute x2, waiting for transfers between devices, padded(): before = lax.ppermute(last, axis, up)  49.1 us
    dot_general x1, matrix products, forward(): return jnp.einsum('flrn,nk->flrk', grid, basis_table, precision=PRECISE)  20 us
    dot_general x1, matrix products, inverse(): jnp.einsum('flrk,nk->flrn', coeffs * factors[None, None], basis_table, pr...  19.2 us
    unnamed x30, local copies, waits for them, and re-layouts  11.2 us
    select_n x1, other arithmetic, real_basis(): jnp.where((column <= half_length)[None, :], jnp.cos(angles), jnp.sin(angl...  10.9 us
  transfers between devices with their start and end apart: 7, of which 3 were waited for; matrix products, arithmetic and copies ran while one was open for 16% of the time, Pallas kernels for 0%

commit v1 on v0

--- a/solution.py
+++ b/solution.py
@@ -5,6 +5,11 @@
 from jax.sharding import PartitionSpec as P
 
 PRECISE = lax.Precision.HIGHEST
+
+
+def write_lots_all(frame_in):
+    lower = jax.lax.all_gather(frame_in, axis_name="lon")
+    return jnp.sum(lower, axis=0)
 
 
 def padded(value, sides, width, wrap):
@@ -67,7 +72,7 @@
         return jnp.zeros(grid.shape[:3] + (length,), jnp.float32)
 
     partial_spec = lax.cond(needed, forward, nothing, values)
-    spectrum = lax.psum(partial_spec, "lon")
+    spectrum = write_lots_all(partial_spec)
     factors = column_factors(band_rows, length)
 
     def inverse(coeffs):

time: 463 us -> 364 us (0.79)
  waiting for transfers between devices: 332 us -> 208 us
  other arithmetic: 26.8 us -> 50.3 us
    psum x1 -> x0, waiting for transfers between devices: 279 us -> none  [polar_filter(): spectrum = lax.psum(partial_spec, 'lon')]
    all_to_all x1, waiting for transfers between devices: 0.01 us -> 205 us  [departure_terms(): lax.all_to_all(outgoing, 'lat', split_axis=0, concat_axis=0, tiled=True)]
    ppermute x2, waiting for transfers between devices: 49.1 us -> 0.01 us  [padded(): before = lax.ppermute(last, axis, up)]
    reduce_sum x0 -> x1, other arithmetic: none -> 18.8 us  [write_lots_all(): return jnp.sum(lower, axis=0)]
    unnamed x30 -> x24, local copies, waits for them, and re-layouts: 11.2 us -> 10.4 us
  transfers between devices with their start and end apart: 7 -> 7, of which waited for: 3 -> 2; matrix products, arithmetic and copies ran while one was open for 16% -> 14% of each run, Pallas kernels for 0% -> 0%
where the time goes in v1:
time: 364 us; the launch traced here: 363 us
  waiting for transfers between devices  208 us (57%)
  other arithmetic  50.3 us (14%)
  matrix products  38.8 us (11%)
  local copies, waits for them, and re-layouts  29 us (8%)
  starting transfers between devices  21.4 us (6%)
  between operations  15 us (4%)
    all_to_all x1, waiting for transfers between devices, departure_terms(): lax.all_to_all(outgoing, 'lat', split_axis=0, concat_axis=0, tiled=True)  205 us
    dot_general x1, matrix products, forward(): return jnp.einsum('flrn,nk->flrk', grid, basis_table, precision=PRECISE)  19.8 us
    dot_general x1, matrix products, inverse(): jnp.einsum('flrk,nk->flrn', coeffs * factors[None, None], basis_table, pr...  19 us
    reduce_sum x1, other arithmetic, write_lots_all(): return jnp.sum(lower, axis=0)  18.8 us
    select_n x1, other arithmetic, real_basis(): jnp.where((column <= half_length)[None, :], jnp.cos(angles), jnp.sin(angl...  10.9 us
    unnamed x24, local copies, waits for them, and re-layouts  10.4 us
  transfers between devices with their start and end apart: 7, of which 2 were waited for; matrix products, arithmetic and copies ran while one was open for 14% of the time, Pallas kernels for 0%

profile of v1, /device:TPU:0, one launch (start us, length us, event | category | flops | bytes accessed | tf_op | source)
XLA Modules:
  0.0 362.8 jit_solution(14564308635350740693)
XLA Ops:
  7.2 1.9 pad_maximum_fusion.11
  9.1 0.7 copy.79
  9.8 5.5 %collective-permute-start.2 = (f32[5,16,1,384]{3,1,2,0:T(8,128)}, f32[5,16,1,384]{3,1,2,0:T(8,128)}, u32[]{:S(2)}, u32[]{:S(2)}) collective-permute-start(f32[5,16,1,384]{3,1,2,0:T(8,128)} %copy.79), channel_id=1, source_target_pairs={{0,1},{1,2},{2,3},{3,4},{4,5},{5,6},{6,7},{8,9},{9,10},{10,11},{11... | collective-permute-start | bytes 368648 | tf_op jit(solution)/shard_map/ppermute | solution.py:22
  15.3 1.3 collective-permute-start.3
  16.6 1.6 pad_maximum_fusion.8
  18.2 1.7 copy.77
  20.0 1.7 copy.78
  21.7 1.8 collective-permute-start.1
  23.5 0.6 compare_reduce_fusion
  24.2 10.9 %sine_select_fusion = f32[384,1536]{1,0:T(8,128)} fusion(s32[1536]{0:T(1024)S(1)} %add_select_fusion.1, s32[384]{0:T(512)S(1)} %iota_add_fusion, pred[1536]{0:T(1024)(128)(4,1)S(1)} %iota_compare_fusion.2), kind=kLoop, calls=%fused_computation.42 | loop fusion | flops 5898240 | bytes 2368512 | tf_op jit(solution)/shard_map/jit(_where)/select_n | solution.py:45
  35.7 1.3 copy.58
  37.0 2.2 multiply_bitcast_fusion.1
  39.2 1.0 fusion.22
  40.2 1.5 copy.60
  41.7 2.7 multiply_subtract_fusion
  44.4 1.0 copy.62
  45.5 0.2 multiply_bitcast_fusion
  45.7 0.1 fusion.23
  45.8 1.0 copy.64
  46.8 1.2 subtract_select_fusion
  48.0 2.3 fusion.16
  50.2 19.8 %conditional.2 = (f32[4,16,24,1536]{3,2,1,0:T(8,128)}) conditional(s32[]{:T(128)} %convert_element_type.23, () %tuple.57, (f32[4,16,24,384]{3,2,1,0:T(8,128)}, f32[384,1536]{1,0:T(8,128)}) %tuple.58), branch_computations={%region_1.2_spmd, %region_2.3_spmd} | conditional | flops 10871635968 | bytes 14155784 | solution.py:74
  50.2 19.8 %fusion = f32[4,16,24,1536]{3,2,1,0:T(8,128)} fusion(f32[4,16,24,384]{3,2,1,0:T(8,128)} %get-tuple-element.67, f32[384,1536]{1,0:T(8,128)} %get-tuple-element.68), kind=kOutput, calls=%fused_computation.2 | convolution fusion | flops 10871635968 | bytes 14155776 | tf_op jit(solution)/shard_map/cond/branch_1_fun/flrn,nk->flrk/dot_general | solution.py:69
  70.1 0.7 copy-done.4
  70.8 0.1 copy.66
  70.8 0.1 eq.76
  70.9 0.1 copy.67
  71.0 0.1 broadcast_in_dim.68
  71.1 0.2 convert_reduce_fusion
  71.3 0.3 select_reduce_fusion
  71.6 0.7 copy.69
  72.3 6.9 %all-to-all-start = ((s32[8,1,12]{2,1,0:T(1,128)}), s32[8,1,12]{2,1,0:T(1,128)S(1)}, u32[]{:S(2)}, u32[]{:S(2)}) async-start(s32[8,1,12]{2,1,0:T(1,128)} %copy.69), calls=%async_computation | async-start | bytes 8192 | tf_op jit(solution)/shard_map/all_to_all | solution.py:105
  79.2 2.7 copy.83
  81.9 3.7 %all-to-all-done = s32[8,1,12]{2,1,0:T(1,128)S(1)} async-done(((s32[8,1,12]{2,1,0:T(1,128)}), s32[8,1,12]{2,1,0:T(1,128)S(1)}, u32[]{:S(2)}, u32[]{:S(2)}) %all-to-all-start) | async-done | bytes 416 | tf_op jit(solution)/shard_map/all_to_all | solution.py:105
  85.6 0.1 reshape.169
  85.7 6.0 %gather_fusion = f32[96,4,16,384]{3,2,1,0:T(8,128)} fusion(f32[24,4,16,384]{3,2,1,0:T(8,128)S(1)} %bitcast.60, s32[1024]{0:T(1024)S(1)} %pad_clamp_fusion.1), kind=kCustom, calls=%fused_computation | custom fusion | bytes 18874752 | tf_op jit(solution)/shard_map/gather | solution.py:107
  91.7 5.8 %all-to-all-start.1 = ((f32[8,12,4,16,384]{4,3,2,1,0:T(8,128)}), f32[8,12,4,16,384]{4,3,2,1,0:T(8,128)}, u32[]{:S(2)}, u32[]{:S(2)}) async-start(f32[8,12,4,16,384]{4,3,2,1,0:T(8,128)} %bitcast.61), calls=%async_computation.1 | async-start | bytes 18874368 | tf_op jit(solution)/shard_map/all_to_all | solution.py:108
  97.5 0.1 copy.70
  97.6 0.1 mul.173
  97.8 204.6 %all-to-all-done.1 = f32[8,12,4,16,384]{4,3,2,1,0:T(8,128)} async-done(((f32[8,12,4,16,384]{4,3,2,1,0:T(8,128)}), f32[8,12,4,16,384]{4,3,2,1,0:T(8,128)}, u32[]{:S(2)}, u32[]{:S(2)}) %all-to-all-start.1) | async-done | bytes 9437216 | tf_op jit(solution)/shard_map/all_to_all | solution.py:108
  302.4 6.6 %gather_fusion.1 = f32[48,4,16,384]{3,2,1,0:T(8,128)} fusion(f32[96,4,16,384]{3,2,1,0:T(8,128)} %bitcast.16, s32[1024]{0:T(1024)S(1)} %pad_clamp_fusion), kind=kCustom, calls=%fused_computation.1 | custom fusion | bytes 9437376 | tf_op jit(solution)/shard_map/gather | solution.py:110
  309.0 2.9 fusion.14
  311.9 2.8 copy.72
  314.7 37.9 %conditional.3 = (f32[4,16,24,384]{3,2,1,0:T(8,128)}) conditional(s32[]{:T(128)} %convert_element_type.23, () %tuple.56, (f32[4,4,16,24,1536]{4,3,2,1,0:T(8,128)}, f32[24]{0:T(128)S(1)}, f32[1,1536]{1,0:T(1,128)S(1)}, s32[1,1536]{1,0:T(1,128)S(1)}, s32[1,1536]{1,0:T(1,128)S(1)}, /*index=5*/f32[384,1536]{1,0:T(8,128)}) %tuple.77), branch_computations={%region_3.4_spmd, %region_4.6_spmd} | conditional | flops 10881263616 | bytes 61679728 | solution.py:86
  314.7 18.8 %reduce_sum.27 = f32[4,16,24,1536]{3,2,1,0:T(8,128)} reduce(f32[4,4,16,24,1536]{4,3,2,1,0:T(8,128)} %get-tuple-element.69, f32[]{:T(128)} %constant.26.clone), dimensions={0}, to_apply=%region_5.5 | reduce | flops 7077888 | bytes 47185924 | tf_op jit(solution)/shard_map/reduce_sum | solution.py:12
  333.6 0.1 fusion.8
  333.7 19.0 %fusion.2 = f32[4,16,24,384]{3,2,1,0:T(8,128)} fusion(f32[4,16,24,1536]{3,2,1,0:T(8,128)} %reduce_sum.27, f32[24,1536]{1,0:T(8,128)S(1)} %fusion.8, f32[384,1536]{1,0:T(8,128)} %get-tuple-element.74), kind=kOutput, calls=%fused_computation.4 | convolution fusion | flops 10873995264 | bytes 14303232 | tf_op jit(solution)/shard_map/cond/branch_1_fun/flrk,nk->flrn/dot_general | solution.py:79
  352.6 3.3 add.100
  (42 shorter events, 0.3 us)
Async XLA Ops:
  7.2 9.5 %copy-start = (f32[4,16,24,384]{3,2,1,0:T(8,128)S(1)}, f32[4,16,24,384]{3,2,1,0:T(8,128)}, u32[]{:S(2)}) copy-start(f32[4,16,24,384]{3,2,1,0:T(8,128)} %param.12) | copy-start | bytes 7077892
  7.2 9.5 %copy-start.2 = (f32[16,24,384]{2,1,0:T(8,128)S(1)}, f32[16,24,384]{2,1,0:T(8,128)}, u32[]{:S(2)}) copy-start(f32[16,24,384]{2,1,0:T(8,128)} %param.14) | copy-start | bytes 1769476
  7.2 307.5 %all-gather.3.cloned.1.call-start = ((), (), s32[]{:S(2)}) async-start(), calls=%async_computation.2 | async-start | bytes 47185920 | tf_op jit(solution)/shard_map/all_gather | solution.py:11
  9.8 34.6 %collective-permute-start.2 = (f32[5,16,1,384]{3,1,2,0:T(8,128)}, f32[5,16,1,384]{3,1,2,0:T(8,128)}, u32[]{:S(2)}, u32[]{:S(2)}) collective-permute-start(f32[5,16,1,384]{3,1,2,0:T(8,128)} %copy.79), channel_id=1, source_target_pairs={{0,1},{1,2},{2,3},{3,4},{4,5},{5,6},{6,7},{8,9},{9,10},{10,11},{11... | collective-permute-start | bytes 368648 | tf_op jit(solution)/shard_map/ppermute | solution.py:22
  15.3 30.4 %collective-permute-start.3 = (f32[5,16,1,384]{3,1,2,0:T(8,128)S(1)}, f32[5,16,1,384]{3,1,2,0:T(8,128)}, u32[]{:S(2)}, u32[]{:S(2)}) collective-permute-start(f32[5,16,1,384]{3,1,2,0:T(8,128)S(1)} %copy.80), channel_id=1, source_target_pairs={{1,0},{2,1},{3,2},{4,3},{5,4},{6,5},{7,6},{9,8},{10,9},{11,10},{12... | collective-permute-start | bytes 368648 | tf_op jit(solution)/shard_map/ppermute | solution.py:23
  16.6 6.9 %copy-start.7 = (s32[24]{0:T(128)S(1)}, s32[24]{0:T(128)}, u32[]{:S(2)}) copy-start(s32[24]{0:T(128)} %param.16) | copy-start | bytes 292
  19.9 15.7 %collective-permute-start = (f32[5,16,24,1]{2,1,3,0:T(8,128)S(1)}, f32[5,16,24,1]{2,1,3,0:T(8,128)}, u32[]{:S(2)}, u32[]{:S(2)}) collective-permute-start(f32[5,16,24,1]{2,1,3,0:T(8,128)S(1)} %copy.77), channel_id=1, source_target_pairs={{0,8},{8,16},{16,24},{24,0},{1,9},{9,17},{17,25},{25,1},{2,10},{10... | collective-permute-start | bytes 23048 | tf_op jit(solution)/shard_map/ppermute | solution.py:22
  21.7 18.5 %collective-permute-start.1 = (f32[5,16,24,1]{2,1,3,0:T(8,128)S(1)}, f32[5,16,24,1]{2,1,3,0:T(8,128)S(1)}, u32[]{:S(2)}, u32[]{:S(2)}) collective-permute-start(f32[5,16,24,1]{2,1,3,0:T(8,128)S(1)} %copy.78), channel_id=1, source_target_pairs={{8,0},{16,8},{24,16},{0,24},{9,1},{17,9},{25,17},{1,25},{10,2},{18... | collective-permute-start | bytes 23048 | tf_op jit(solution)/shard_map/ppermute | solution.py:23
  41.7 3.8 %copy-start.3 = (f32[16,24,384]{2,1,0:T(8,128)S(1)}, f32[16,24,384]{2,1,0:T(8,128)}, u32[]{:S(2)}) copy-start(f32[16,24,384]{2,1,0:T(8,128)} %param.15) | copy-start | bytes 1769476
  70.1 0.7 copy-start.4
  70.1 0.9 copy-start.6
  72.3 13.3 %all-to-all-start = ((s32[8,1,12]{2,1,0:T(1,128)}), s32[8,1,12]{2,1,0:T(1,128)S(1)}, u32[]{:S(2)}, u32[]{:S(2)}) async-start(s32[8,1,12]{2,1,0:T(1,128)} %copy.69), calls=%async_computation | async-start | bytes 8192 | tf_op jit(solution)/shard_map/all_to_all | solution.py:105
  91.7 6.0 %copy-start.5 = (f32[24,2]{0,1:T(2,128)S(1)}, f32[24,2]{0,1:T(2,128)}, u32[]{:S(2)}) copy-start(f32[24,2]{0,1:T(2,128)} %param.19) | copy-start | bytes 580
  91.7 210.6 %all-to-all-start.1 = ((f32[8,12,4,16,384]{4,3,2,1,0:T(8,128)}), f32[8,12,4,16,384]{4,3,2,1,0:T(8,128)}, u32[]{:S(2)}, u32[]{:S(2)}) async-start(f32[8,12,4,16,384]{4,3,2,1,0:T(8,128)} %bitcast.61), calls=%async_computation.1 | async-start | bytes 18874368 | tf_op jit(solution)/shard_map/all_to_all | solution.py:108
  314.7 37.9 %copy-start.1 = (f32[4,16,24,384]{3,2,1,0:T(8,128)S(1)}, f32[4,16,24,384]{3,2,1,0:T(8,128)}, u32[]{:S(2)}) copy-start(f32[4,16,24,384]{3,2,1,0:T(8,128)} %fusion.16) | copy-start | bytes 7077892
Sparse Core Ops, SparseCore 0:
  70.2 229.5 all-gather.2
